TPU v7x, 32 devices: a whole 2x2x4 slice. The times are simulated.
32 devices in a mesh: sample: 16 (over z, x, core), block: 2 (over y).
Axes of the slice: x: 2, y: 2, z: 4, core: 2. Of those that a mesh axis runs over, the one named last changes fastest.
Arguments:
- genotype: int32 [16384, 2000], P('sample', 'block'), may hold values from 0 to 2
- allele_freq: float32 [2000], P('block'), may hold values from 0.05 to 0.5
- phenotype: bfloat16 [16384, 16], P('sample'), may hold values from -6 to 6
- shrinkage: float32 [2], replicated, may hold values from 0.05 to 2
- owner_order: int32 [16], replicated, may hold values from 0 to 15, each once
Outputs:
- predictions: bfloat16 [16, 8, 16384], P('block', None, 'sample')
Inputs may be any that keep to these rules, and one draw needn't show every extreme that they name: `owner_order`: each phenotype appears once.
All inputs are finite; a program needn't handle non-finite values.
Results may differ from a plain program's by a relative error of at most 0.0056.
Values may be sent and summed in bfloat16 or wider, within the bound.
No kernel may reach another device: no remote copies, remote signals or barrier semaphores. Data moves between devices by JAX's collectives and lax.ppermute only.
A program may use at most 128 MiB of HBM per device.

v0:
```python
import jax
import jax.numpy as jnp
from jax import lax
from jax.sharding import PartitionSpec as P

SNPS = 500
FOLDS = 5
PANEL = 128
HIGH = lax.Precision.HIGHEST


def standardize(genotype, allele_freq):
    spread = jnp.sqrt(2.0 * allele_freq * (1.0 - allele_freq))
    return ((genotype.astype(jnp.float32) - 2.0 * allele_freq) / spread).astype(jnp.bfloat16)


def predict(columns, weights):
    stacked = jnp.transpose(weights, (2, 0, 1)).reshape(-1, weights.shape[1])
    product = lax.dot_general(
        stacked, columns, (((1,), (1,)), ((), ())), preferred_element_type=jnp.float32
    )
    return product.astype(jnp.bfloat16).reshape(
        weights.shape[2], weights.shape[0], columns.shape[0]
    )


def inner_products(left_cols, right_cols):
    return lax.dot_general(
        left_cols, right_cols, (((0,), (0,)), ((), ())), preferred_element_type=jnp.float32
    )


def tile_pairs(panels):
    pairs = []
    for row_tile in range(panels):
        for col_tile in range(row_tile, panels):
            pairs.append((row_tile, col_tile))
    return pairs


def tile_grams(left_cols, right_cols, panels):
    tile_list = []
    for row_tile, col_tile in tile_pairs(panels):
        first = left_cols[:, row_tile * PANEL : (row_tile + 1) * PANEL]
        second = right_cols[:, col_tile * PANEL : (col_tile + 1) * PANEL]
        tile_list.append(inner_products(first, second))
    return jnp.stack(tile_list)


def mm(spec, left, right):
    return jnp.einsum(spec, left, right, precision=HIGH, preferred_element_type=jnp.float32)


def block_solve(tiles, target, panels):
    pairs = tile_pairs(panels)
    upper = {pair: tiles[:, index] for index, pair in enumerate(pairs)}
    eye = jnp.broadcast_to(jnp.eye(PANEL, dtype=jnp.float32), (tiles.shape[0], PANEL, PANEL))
    lower = {}
    inverse = {}
    for p in range(panels):
        factor = jnp.linalg.cholesky(upper[p, p])
        inv = lax.linalg.triangular_solve(factor, eye, left_side=True, lower=True)
        inverse[p] = inv
        for q in range(p + 1, panels):
            lower[q, p] = mm("sji,skj->sik", upper[p, q], inv)
        for r in range(p + 1, panels):
            for q in range(r, panels):
                upper[r, q] = upper[r, q] - mm("sik,sjk->sij", lower[r, p], lower[q, p])
    forward = []
    for p in range(panels):
        rhs = target[:, p * PANEL : (p + 1) * PANEL]
        for q in range(p):
            rhs = rhs - mm("sij,sjc->sic", lower[p, q], forward[q])
        forward.append(mm("sij,sjc->sic", inverse[p], rhs))
    backward = [None] * panels
    for p in reversed(range(panels)):
        rhs = forward[p]
        for q in range(p + 1, panels):
            rhs = rhs - mm("sji,sjc->sic", lower[q, p], backward[q])
        backward[p] = mm("sji,sjc->sic", inverse[p], rhs)
    return jnp.concatenate(backward, axis=1)


def shared_solve(summed_grams, summed_crosses, shrinkage, counts, panels):
    member_count = summed_grams.shape[1]
    ridge_count = shrinkage.shape[0]
    systems = FOLDS * member_count * ridge_count
    devices = lax.axis_size("sample")
    share = -(-systems // devices)
    owned_ids = lax.axis_index("sample") * share + lax.broadcasted_iota(jnp.int32, (share,), 0)
    owned_ids = jnp.minimum(owned_ids, systems - 1)
    pair_ids = owned_ids // ridge_count
    ridge_ids = owned_ids % ridge_count
    fold_ids = pair_ids // member_count
    member_ids = pair_ids % member_count
    fold_axis = jnp.arange(FOLDS, dtype=jnp.int32)[:, None, None]
    member_axis = jnp.arange(member_count, dtype=jnp.int32)[None, :, None]
    keep = jnp.logical_and(
        fold_axis != fold_ids[None, None, :], member_axis == member_ids[None, None, :]
    )
    keep = keep.astype(jnp.float32)
    rest_tiles = jnp.einsum("kms,kmtij->stij", keep, summed_grams, precision=HIGH)
    rest_crosses = jnp.einsum("kms,kmic->sic", keep, summed_crosses, precision=HIGH)
    chosen_counts = jnp.take(counts, fold_ids, axis=0)
    ridge = jnp.take(shrinkage, ridge_ids, axis=0)
    width = rest_tiles.shape[-1]
    diag_ids = [
        index
        for index, (row_tile, col_tile) in enumerate(tile_pairs(panels))
        if row_tile == col_tile
    ]
    is_diag = jnp.zeros((len(tile_pairs(panels)),), jnp.float32).at[jnp.array(diag_ids)].set(1.0)
    position = lax.broadcasted_iota(jnp.int32, (panels, width), 1) + PANEL * lax.broadcasted_iota(
        jnp.int32, (panels, width), 0
    )
    padded = (position >= SNPS).astype(jnp.float32)
    pad_diag = (
        jnp.zeros((len(tile_pairs(panels)), width), jnp.float32).at[jnp.array(diag_ids)].set(padded)
    )
    identity = jnp.eye(width, dtype=jnp.float32)
    diag_add = (
        ridge[:, None, None] * is_diag[None, :, None]
        + (1.0 - ridge[:, None, None]) * pad_diag[None, :, :]
    )
    system = rest_tiles / chosen_counts[:, None, None, None] + diag_add[:, :, :, None] * identity
    target = rest_crosses / chosen_counts[:, None, None]
    solved = block_solve(system, target, panels)[:, :SNPS].astype(jnp.bfloat16)
    collected = lax.all_gather(solved, "sample", axis=0, tiled=True)
    return collected[:systems].reshape(FOLDS, member_count, ridge_count, SNPS, -1)


def shards(genotype, allele_freq, phenotype, shrinkage, owner_order):
    sample_rows = genotype.shape[0]
    total_rows = sample_rows * lax.axis_size("sample")
    scaled = standardize(genotype, allele_freq)
    ordered = jnp.take(phenotype, owner_order, axis=1)
    local_blocks = allele_freq.shape[0] // SNPS
    panels = -(-SNPS // PANEL)
    padded_width = panels * PANEL
    column_sets = [scaled[:, member * SNPS : (member + 1) * SNPS] for member in range(local_blocks)]
    bounds = [-(-(k * total_rows) // FOLDS) for k in range(FOLDS + 1)]
    counts = jnp.array(
        [float(total_rows - (bounds[k + 1] - bounds[k])) for k in range(FOLDS)], dtype=jnp.float32
    )
    start_row = lax.axis_index("sample") * sample_rows
    row_ids = start_row + lax.broadcasted_iota(jnp.int32, (sample_rows,), 0)
    fold_of = row_ids * FOLDS // total_rows
    first_fold = start_row * FOLDS // total_rows
    slot_folds = [first_fold, first_fold + 1]
    slot_masks = [fold_of == slot_folds[0], fold_of == slot_folds[1]]
    picked = jnp.minimum(jnp.stack(slot_folds), FOLDS - 1)
    fold_ids = jnp.arange(FOLDS, dtype=jnp.int32)
    tile_count = len(tile_pairs(panels))

    def fold_partials(member):
        columns = jnp.pad(column_sets[member], ((0, 0), (0, padded_width - SNPS)))
        gram_total = jnp.zeros((FOLDS, tile_count, PANEL, PANEL), jnp.float32)
        cross_total = jnp.zeros((FOLDS, padded_width, ordered.shape[1]), jnp.float32)
        for slot in range(2):
            masked = jnp.where(slot_masks[slot][:, None], columns, jnp.zeros_like(columns))
            selector = (fold_ids == slot_folds[slot]).astype(jnp.float32)
            gram_total = (
                gram_total
                + selector[:, None, None, None] * tile_grams(masked, columns, panels)[None]
            )
            cross_total = (
                cross_total + selector[:, None, None] * inner_products(masked, ordered)[None]
            )
        return (gram_total, cross_total)

    def weights_for(members):
        parts = [fold_partials(member) for member in members]
        grams = jnp.stack([item[0] for item in parts], axis=1)
        crosses = jnp.stack([item[1] for item in parts], axis=1)
        summed_grams, summed_crosses = lax.psum((grams, crosses), "sample")
        every_weights = shared_solve(summed_grams, summed_crosses, shrinkage, counts, panels)
        return jnp.take(every_weights, picked, axis=0)

    def fold_predictions(member, slot_weights):
        columns = column_sets[member]
        lower = predict(columns, slot_weights[0])
        upper = predict(columns, slot_weights[1])
        return jnp.where(slot_masks[1][None, None, :], upper, lower)

    weights = weights_for(list(range(local_blocks)))
    local_preds = jnp.concatenate(
        [fold_predictions(member, weights[:, member]) for member in range(local_blocks)], axis=1
    )
    return lax.all_to_all(local_preds, "block", split_axis=0, concat_axis=1, tiled=True)


def solution(mesh):
    in_specs = (P("sample", "block"), P("block"), P("sample", None), P(), P())
    out_specs = P("block", None, "sample")
    return jax.shard_map(shards, mesh=mesh, in_specs=in_specs, out_specs=out_specs, check_vma=False)
```

profile of v0, /device:TPU:0, one launch (start us, length us, event | category | flops | bytes accessed | tf_op | source)
XLA Modules:
  0.0 510.8 jit_solution(4476587535390059192)
XLA Ops:
  8.6 2.7 divide_convert_fusion
  25.3 1.4 multiply_add_fusion.1
  26.7 4.9 pad_maximum_fusion
  37.5 205.3 %all-reduce.4.cloned.1.call-done = (f32[5,2,10,128,128]{4,0,1,3,2:T(8,128)}, f32[5,2,512,16]{2,0,1,3:T(8,128)}) async-done(((f32[5,2,10,128,128]{4,0,1,3,2:T(8,128)}, f32[5,2,512,16]{2,0,1,3:T(8,128)}), (f32[5,2,10,128,128]{4,0,1,3,2:T(8,128)}, f32[5,2,512,16]{2,0,1,3:T(8,128)})) %all-reduce.4.cloned.1.call-update) | async-done | bytes 6881296 | tf_op jit(solution)/shard_map/psum | solution.py:175
  242.8 10.3 %convolution_bitcast_fusion = f32[2,10,128,128]{3,0,2,1:T(2,128)S(1)} fusion(f32[5,2,10,128,128]{4,0,1,3,2:T(8,128)} %get-tuple-element.6, pred[2,2]{1,0:T(4,128)(4,1)S(1)} %iota_compare_fusion.3, pred[5,2]{0,1:T(4,128)(4,1)S(1)} %iota_compare_fusion.4), kind=kOutput, calls=%fused_computation.9 | convolution fusion | flops 39321620 | bytes 7864334 | tf_op jit(solution)/shard_map/kms,kmtij->stij/dot_general | solution.py:102
  253.1 2.6 copy.154
  255.7 1.7 multiply_add_fusion.2
  258.1 1.7 copy.155
  259.8 1.6 fusion.97
  261.4 24.9 %custom-call.12 = f32[2,128,128]{2,1,0:T(8,128)} custom-call(f32[2,128,128]{2,1,0:T(8,128)} %fusion.97), custom_call_target="Cholesky" | custom-call | tf_op jit(solution)/shard_map/jit(cholesky)/cholesky | solution.py:61
  287.3 1.6 select_bitcast_fusion.3
  289.0 21.1 %custom-call.13 = f32[2,1,128,128]{2,3,1,0:T(8,128)} custom-call(f32[2,1,128,128]{3,2,1,0:T(8,128)} %select_bitcast_fusion.3), custom_call_target="InvertDiagBlocksLowerTriangular" | custom-call | tf_op jit(solution)/shard_map/triangular_solve/custom-call.0 | solution.py:62
  310.1 1.3 fusion.107
  311.8 1.4 fusion.95
  313.2 1.3 fusion.96
  314.5 1.5 convolution_bitcast_fusion.1
  317.1 1.3 convolution_subtract_fusion.9
  320.8 1.1 convolution_subtract_fusion.5
  322.8 23.9 %custom-call.14 = f32[2,128,128]{2,1,0:T(8,128)S(1)} custom-call(f32[2,128,128]{2,1,0:T(8,128)S(1)} %fusion.106), custom_call_target="Cholesky" | custom-call | tf_op jit(solution)/shard_map/jit(cholesky)/cholesky | solution.py:61
  346.9 19.7 %custom-call.15 = f32[2,1,128,128]{2,3,1,0:T(8,128)S(1)} custom-call(f32[2,1,128,128]{3,2,1,0:T(8,128)S(1)} %select_bitcast_fusion.2), custom_call_target="InvertDiagBlocksLowerTriangular" | custom-call | tf_op jit(solution)/shard_map/triangular_solve/custom-call.0 | solution.py:62
  369.0 1.0 convolution_subtract_fusion.19
  370.0 1.3 convolution_subtract_fusion.3
  371.7 1.1 convolution_subtract_fusion.1
  372.9 23.5 %custom-call.16 = f32[2,128,128]{2,1,0:T(8,128)S(1)} custom-call(f32[2,128,128]{2,1,0:T(8,128)S(1)} %fusion.103), custom_call_target="Cholesky" | custom-call | tf_op jit(solution)/shard_map/jit(cholesky)/cholesky | solution.py:61
  396.6 19.8 %custom-call.17 = f32[2,1,128,128]{2,3,1,0:T(8,128)S(1)} custom-call(f32[2,1,128,128]{3,2,1,0:T(8,128)S(1)} %select_bitcast_fusion.1), custom_call_target="InvertDiagBlocksLowerTriangular" | custom-call | tf_op jit(solution)/shard_map/triangular_solve/custom-call.0 | solution.py:62
  417.6 1.3 convolution_subtract_fusion
  419.7 1.6 fusion.100
  421.2 24.3 %custom-call.18 = f32[2,128,128]{2,1,0:T(8,128)S(1)} custom-call(f32[2,128,128]{2,1,0:T(8,128)} %fusion.100), custom_call_target="Cholesky" | custom-call | tf_op jit(solution)/shard_map/jit(cholesky)/cholesky | solution.py:61
  446.4 20.5 %custom-call.19 = f32[2,1,128,128]{2,3,1,0:T(8,128)S(1)} custom-call(f32[2,1,128,128]{3,2,1,0:T(8,128)} %select_bitcast_fusion), custom_call_target="InvertDiagBlocksLowerTriangular" | custom-call | tf_op jit(solution)/shard_map/triangular_solve/custom-call.0 | solution.py:62
  467.3 1.0 convolution_subtract_fusion.16
  471.0 21.9 %all_gather.3 = bf16[32,500,16]{1,2,0:T(8,128)(2,1)S(1)} all-gather(bf16[2,500,16]{1,2,0:T(8,128)(2,1)S(1)} %pad_maximum_fusion.3), channel_id=1, replica_groups=mesh['sample'=16,'block'=2] {'sample'}, dimensions={0}, use_global_device_ids=true | all-gather | bytes 544000 | tf_op jit(solution)/shard_map/all_gather | solution.py:128
  496.0 7.0 %all_to_all.18 = bf16[16,4,1024]{2,1,0:T(4,128)(2,1)S(1)} all-to-all(bf16[16,4,1024]{2,1,0:T(4,128)(2,1)S(1)} %pad_maximum_fusion.2), channel_id=1, replica_groups=mesh['sample'=16,'block'=2] {'block'}, dimensions={0} | all-to-all | bytes 262144 | tf_op jit(solution)/shard_map/all_to_all | solution.py:189
  (185 shorter events, 40.8 us)
Async XLA Ops:
  6.5 5.1 copy-start
  6.5 236.2 %all-reduce.4.cloned.1.call-start = ((), (), s32[]{:S(2)}) async-start(), calls=%async_computation.1 | async-start | bytes 22020096 | tf_op jit(solution)/shard_map/psum | solution.py:175
  7.9 5.1 copy-start.10
  12.2 0.8 copy-start.15
  31.6 0.8 copy-start.2
  31.6 1.5 copy-start.1
  31.6 5.1 %copy-start.16 = (f32[10]{0:T(128)S(1)}, f32[10]{0:T(128)}, u32[]{:S(2)}) copy-start(f32[10]{0:T(128)} %constant.196) | copy-start | bytes 124
  31.7 211.1 %copy-start.9 = (f32[128,128]{0,1:T(8,128)}, f32[128,128]{0,1:T(8,128)S(1)}, u32[]{:S(2)}) copy-start(f32[128,128]{0,1:T(8,128)S(1)} %fusion.125) | copy-start | bytes 196612
  36.0 217.1 %copy-start.12 = (pred[2,2]{1,0:T(4,128)(4,1)}, pred[2,2]{1,0:T(4,128)(4,1)S(1)}, u32[]{:S(2)}) copy-start(pred[2,2]{1,0:T(4,128)(4,1)S(1)} %iota_compare_fusion.3) | copy-start | bytes 16
  36.1 217.0 %copy-start.13 = (pred[5,2]{0,1:T(4,128)(4,1)}, pred[5,2]{0,1:T(4,128)(4,1)S(1)}, u32[]{:S(2)}) copy-start(pred[5,2]{0,1:T(4,128)(4,1)S(1)} %iota_compare_fusion.4) | copy-start | bytes 34
  255.7 54.3 %copy-start.7 = (f32[128,128]{1,0:T(8,128)S(1)}, f32[128,128]{1,0:T(8,128)}, u32[]{:S(2)}) copy-start(f32[128,128]{1,0:T(8,128)} %copy.156) | copy-start | bytes 196612
  257.4 53.9 %copy-start.3 = (f32[2,10,128,128]{2,3,0,1:T(8,128)}, f32[2,10,128,128]{2,3,0,1:T(8,128)S(1)}, u32[]{:S(2)}) copy-start(f32[2,10,128,128]{2,3,0,1:T(8,128)S(1)} %multiply_add_fusion.2) | copy-start | bytes 3932164
  311.4 9.4 %copy-start.5 = (f32[2,128,128]{2,1,0:T(8,128)}, f32[2,128,128]{2,1,0:T(8,128)S(1)}, u32[]{:S(2)}) copy-start(f32[2,128,128]{2,1,0:T(8,128)S(1)} %fusion.107) | copy-start | bytes 393220
  311.8 7.3 %copy-start.4 = (f32[2,10,128,128]{2,3,0,1:T(8,128)S(1)}, f32[2,10,128,128]{2,3,0,1:T(8,128)}, u32[]{:S(2)}) copy-start(f32[2,10,128,128]{2,3,0,1:T(8,128)} %copy-done.3) | copy-start | bytes 3932164
  318.7 47.9 %copy-start.8 = (f32[128,128]{1,0:T(8,128)S(1)}, f32[128,128]{1,0:T(8,128)}, u32[]{:S(2)}) copy-start(f32[128,128]{1,0:T(8,128)} %copy.156) | copy-start | bytes 196612
  417.3 53.5 %copy-start.6 = (f32[2,128,128]{2,1,0:T(8,128)S(1)}, f32[2,128,128]{2,1,0:T(8,128)}, u32[]{:S(2)}) copy-start(f32[2,128,128]{2,1,0:T(8,128)} %copy-done.5) | copy-start | bytes 393220
  470.0 23.6 %copy-start.14 = (pred[2]{0:T(512)(128)(4,1)S(1)}, pred[2]{0:T(512)(128)(4,1)}, u32[]{:S(2)}) copy-start(pred[2]{0:T(512)(128)(4,1)} %compare_and_fusion.1) | copy-start | bytes 10
  494.8 0.9 copy-start.11
Sparse Core Ops, SparseCore 0:
  31.8 210.9 all-reduce.3
where the time goes:
time: 518 us; the launch traced here: 511 us
  waiting for transfers between devices  205 us (40%)
  other arithmetic  204 us (39%)
  matrix products  46.8 us (9%)
  blocking collectives  28.9 us (6%)
  between operations  14.5 us (3%)
  local copies, waits for them, and re-layouts  10.7 us (2%)
    psum x1, waiting for transfers between devices, weights_for(): summed_grams, summed_crosses = lax.psum((grams, crosses), 'sample')  205 us
    another operation x13, other arithmetic, block_solve(): factor = jnp.linalg.cholesky(upper[p, p])  98 us
    another operation x9, other arithmetic, block_solve(): inv = lax.linalg.triangular_solve(factor, eye, left_side=True, lower=True)  83.7 us
    all_gather x1, blocking collectives, shared_solve(): collected = lax.all_gather(solved, 'sample', axis=0, tiled=True)  21.9 us
    dot_general x36, matrix products, mm(): jnp.einsum(spec, left, right, precision=HIGH, preferred_element_type=jnp....  20.4 us
    dot_general x44, matrix products, inner_products(): lax.dot_general(left_cols, right_cols, (((0,), (0,)), ((), ())), preferre...  10.8 us
  transfers between devices with their start and end apart: 1, of which 1 were waited for; matrix products, arithmetic and copies ran while one was open for 1% of the time, Pallas kernels for 0%

commit v1 on v0

--- a/solution.py
+++ b/solution.py
@@ -125,7 +125,29 @@
     system = rest_tiles / chosen_counts[:, None, None, None] + diag_add[:, :, :, None] * identity
     target = rest_crosses / chosen_counts[:, None, None]
     solved = block_solve(system, target, panels)[:, :SNPS].astype(jnp.bfloat16)
-    collected = lax.all_gather(solved, "sample", axis=0, tiled=True)
+    seen = []
+    dev = 0
+    shares = jax.lax.axis_size("sample")
+    while dev < shares:
+        seen.append((dev, (dev + 1) % shares))
+        dev = dev + 1
+    found = []
+    dev = 0
+    while dev < shares:
+        found.append((dev, (dev - 1) % shares))
+        dev = dev + 1
+    placed, arr_next = ([solved], [solved])
+    for _ in range(shares // 2):
+        step_out = jax.lax.ppermute(placed[-1], "sample", perm=seen)
+        placed.append(step_out)
+    pp = 0
+    while pp < (shares - 1) // 2:
+        top = jax.lax.ppermute(arr_next[-1], "sample", found)
+        arr_next.append(top)
+        pp += 1
+    after = jnp.concatenate([*placed[::-1], *arr_next[1:]], 0)
+    r1 = jax.lax.axis_index("sample")
+    collected = jnp.roll(after, (r1 - shares // 2) * solved.shape[0], 0)
     return collected[:systems].reshape(FOLDS, member_count, ridge_count, SNPS, -1)
 
 

time: 518 us -> 546 us (1.054)
  starting transfers between devices: 0.01 us -> 31.4 us
  blocking collectives: 28.9 us -> 7.01 us
  waiting for transfers between devices: 205 us -> 224 us
    ppermute x0 -> x15, starting transfers between devices: none -> 31.4 us  [the longest x7 31.1 us: shared_solve(): top = jax.lax.ppermute(arr_next[-1], 'sample', found)]
    all_gather x1 -> x0, blocking collectives: 21.9 us -> none  [shared_solve(): collected = lax.all_gather(solved, 'sample', axis=0, tiled=True)]
    ppermute x0 -> x15, waiting for transfers between devices: none -> 17.1 us  [the longest x8 17.1 us: shared_solve(): step_out = jax.lax.ppermute(placed[-1], 'sample', perm=seen)]
  transfers between devices with their start and end apart: 1 -> 16, of which waited for: 1 -> 9; matrix products, arithmetic and copies ran while one was open for 1% -> 1% of each run, Pallas kernels for 0% -> 0%
where the time goes in v1:
time: 546 us; the launch traced here: 539 us
  waiting for transfers between devices  224 us (41%)
  other arithmetic  204 us (37%)
  matrix products  46.8 us (9%)
  starting transfers between devices  31.4 us (6%)
  between operations  14.8 us (3%)
  local copies, waits for them, and re-layouts  10.9 us (2%)
  blocking collectives  7.01 us (1%)
    psum x1, waiting for transfers between devices, weights_for(): summed_grams, summed_crosses = lax.psum((grams, crosses), 'sample')  207 us
    another operation x13, other arithmetic, block_solve(): factor = jnp.linalg.cholesky(upper[p, p])  98 us
    another operation x9, other arithmetic, block_solve(): inv = lax.linalg.triangular_solve(factor, eye, left_side=True, lower=True)  83.7 us
    ppermute x7, starting transfers between devices, shared_solve(): top = jax.lax.ppermute(arr_next[-1], 'sample', found)  31.1 us
    dot_general x36, matrix products, mm(): jnp.einsum(spec, left, right, precision=HIGH, preferred_element_type=jnp....  20.4 us
    ppermute x8, waiting for transfers between devices, shared_solve(): step_out = jax.lax.ppermute(placed[-1], 'sample', perm=seen)  17.1 us
  transfers between devices with their start and end apart: 16, of which 9 were waited for; matrix products, arithmetic and copies ran while one was open for 1% of the time, Pallas kernels for 0%

profile of v1, /device:TPU:0, one launch (start us, length us, event | category | flops | bytes accessed | tf_op | source)
XLA Modules:
  0.0 538.5 jit_solution(6331177492002957270)
XLA Ops:
  8.6 2.7 divide_convert_fusion
  27.3 4.9 pad_maximum_fusion
  36.8 206.6 %all-reduce.4.cloned.1.call-done = (f32[5,2,10,128,128]{4,0,1,3,2:T(8,128)}, f32[5,2,512,16]{2,0,1,3:T(8,128)}) async-done(((f32[5,2,10,128,128]{4,0,1,3,2:T(8,128)}, f32[5,2,512,16]{2,0,1,3:T(8,128)}), (f32[5,2,10,128,128]{4,0,1,3,2:T(8,128)}, f32[5,2,512,16]{2,0,1,3:T(8,128)})) %all-reduce.4.cloned.1.call-update) | async-done | bytes 6881296 | tf_op jit(solution)/shard_map/psum | solution.py:197
  243.4 10.3 %convolution_bitcast_fusion = f32[2,10,128,128]{3,0,2,1:T(2,128)S(1)} fusion(f32[5,2,10,128,128]{4,0,1,3,2:T(8,128)} %get-tuple-element.6, pred[2,2]{1,0:T(4,128)(4,1)S(1)} %iota_compare_fusion.3, pred[5,2]{0,1:T(4,128)(4,1)S(1)} %iota_compare_fusion.4), kind=kOutput, calls=%fused_computation.9 | convolution fusion | flops 39321620 | bytes 7864334 | tf_op jit(solution)/shard_map/kms,kmtij->stij/dot_general | solution.py:102
  253.8 2.6 copy.119
  256.4 1.7 multiply_add_fusion.2
  258.8 1.7 copy.120
  260.4 1.6 fusion.97
  262.0 24.9 %custom-call.12 = f32[2,128,128]{2,1,0:T(8,128)} custom-call(f32[2,128,128]{2,1,0:T(8,128)} %fusion.97), custom_call_target="Cholesky" | custom-call | tf_op jit(solution)/shard_map/jit(cholesky)/cholesky | solution.py:61
  288.0 1.6 select_bitcast_fusion.3
  289.6 21.1 %custom-call.13 = f32[2,1,128,128]{2,3,1,0:T(8,128)} custom-call(f32[2,1,128,128]{3,2,1,0:T(8,128)} %select_bitcast_fusion.3), custom_call_target="InvertDiagBlocksLowerTriangular" | custom-call | tf_op jit(solution)/shard_map/triangular_solve/custom-call.0 | solution.py:62
  323.3 23.9 %custom-call.14 = f32[2,128,128]{2,1,0:T(8,128)S(1)} custom-call(f32[2,128,128]{2,1,0:T(8,128)S(1)} %fusion.106), custom_call_target="Cholesky" | custom-call | tf_op jit(solution)/shard_map/jit(cholesky)/cholesky | solution.py:61
  347.5 19.7 %custom-call.15 = f32[2,1,128,128]{2,3,1,0:T(8,128)S(1)} custom-call(f32[2,1,128,128]{3,2,1,0:T(8,128)S(1)} %select_bitcast_fusion.2), custom_call_target="InvertDiagBlocksLowerTriangular" | custom-call | tf_op jit(solution)/shard_map/triangular_solve/custom-call.0 | solution.py:62
  373.5 23.5 %custom-call.16 = f32[2,128,128]{2,1,0:T(8,128)S(1)} custom-call(f32[2,128,128]{2,1,0:T(8,128)S(1)} %fusion.103), custom_call_target="Cholesky" | custom-call | tf_op jit(solution)/shard_map/jit(cholesky)/cholesky | solution.py:61
  397.2 19.8 %custom-call.17 = f32[2,1,128,128]{2,3,1,0:T(8,128)S(1)} custom-call(f32[2,1,128,128]{3,2,1,0:T(8,128)S(1)} %select_bitcast_fusion.1), custom_call_target="InvertDiagBlocksLowerTriangular" | custom-call | tf_op jit(solution)/shard_map/triangular_solve/custom-call.0 | solution.py:62
  421.8 24.3 %custom-call.18 = f32[2,128,128]{2,1,0:T(8,128)S(1)} custom-call(f32[2,128,128]{2,1,0:T(8,128)} %fusion.100), custom_call_target="Cholesky" | custom-call | tf_op jit(solution)/shard_map/jit(cholesky)/cholesky | solution.py:61
  447.0 20.5 %custom-call.19 = f32[2,1,128,128]{2,3,1,0:T(8,128)S(1)} custom-call(f32[2,1,128,128]{3,2,1,0:T(8,128)} %select_bitcast_fusion), custom_call_target="InvertDiagBlocksLowerTriangular" | custom-call | tf_op jit(solution)/shard_map/triangular_solve/custom-call.0 | solution.py:62
  471.6 6.0 %collective-permute-done = bf16[2,500,16]{1,2,0:T(8,128)(2,1)S(1)} collective-permute-done((bf16[2,500,16]{1,2,0:T(8,128)(2,1)S(1)}, bf16[2,500,16]{1,2,0:T(8,128)(2,1)S(1)}, u32[]{:S(2)}, u32[]{:S(2)}) %collective-permute-start) | collective-permute-done | bytes 32032 | tf_op jit(solution)/shard_map/ppermute | solution.py:141
  477.7 4.4 collective-permute-start.8
  482.1 1.7 collective-permute-done.1
  483.8 4.4 collective-permute-start.9
  488.2 1.6 collective-permute-done.2
  489.8 4.4 collective-permute-start.10
  494.3 1.6 collective-permute-done.3
  495.9 4.4 collective-permute-start.11
  500.3 1.6 collective-permute-done.4
  501.9 4.4 collective-permute-start.12
  506.3 1.6 collective-permute-done.5
  508.2 4.4 collective-permute-start.13
  512.6 1.6 collective-permute-done.6
  514.3 4.5 collective-permute-start.14
  523.7 7.0 %all_to_all.18 = bf16[16,4,1024]{2,1,0:T(4,128)(2,1)S(1)} all-to-all(bf16[16,4,1024]{2,1,0:T(4,128)(2,1)S(1)} %pad_maximum_fusion.2), channel_id=1, replica_groups=mesh['sample'=16,'block'=2] {'block'}, dimensions={0} | all-to-all | bytes 262144 | tf_op jit(solution)/shard_map/all_to_all | solution.py:211
  (243 shorter events, 58.7 us)
Async XLA Ops:
  6.5 5.7 %copy-start = (bf16[1024,16]{0,1:T(8,128)(2,1)S(1)}, bf16[1024,16]{0,1:T(8,128)(2,1)}, u32[]{:S(2)}) copy-start(bf16[1024,16]{0,1:T(8,128)(2,1)} %param.13) | copy-start | bytes 98308
  6.5 236.9 %all-reduce.4.cloned.1.call-start = ((), (), s32[]{:S(2)}) async-start(), calls=%async_computation.1 | async-start | bytes 22020096 | tf_op jit(solution)/shard_map/psum | solution.py:197
  7.9 5.7 %copy-start.10 = (pred[1024]{0:T(1024)(128)(4,1)}, pred[1024]{0:T(1024)(128)(4,1)S(1)}, u32[]{:S(2)}) copy-start(pred[1024]{0:T(1024)(128)(4,1)S(1)} %get-tuple-element.38) | copy-start | bytes 3076
  12.8 0.8 copy-start.14
  32.2 0.9 copy-start.1
  32.2 1.5 copy-start.2
  32.2 3.8 copy-start.15
  32.3 211.1 %copy-start.9 = (f32[128,128]{0,1:T(8,128)}, f32[128,128]{0,1:T(8,128)S(1)}, u32[]{:S(2)}) copy-start(f32[128,128]{0,1:T(8,128)S(1)} %fusion.125) | copy-start | bytes 196612
  35.4 218.4 %copy-start.12 = (pred[2,2]{1,0:T(4,128)(4,1)}, pred[2,2]{1,0:T(4,128)(4,1)S(1)}, u32[]{:S(2)}) copy-start(pred[2,2]{1,0:T(4,128)(4,1)S(1)} %iota_compare_fusion.3) | copy-start | bytes 16
  35.5 218.3 %copy-start.13 = (pred[5,2]{0,1:T(4,128)(4,1)}, pred[5,2]{0,1:T(4,128)(4,1)S(1)}, u32[]{:S(2)}) copy-start(pred[5,2]{0,1:T(4,128)(4,1)S(1)} %iota_compare_fusion.4) | copy-start | bytes 34
  256.4 54.4 %copy-start.7 = (f32[128,128]{1,0:T(8,128)S(1)}, f32[128,128]{1,0:T(8,128)}, u32[]{:S(2)}) copy-start(f32[128,128]{1,0:T(8,128)} %copy.121) | copy-start | bytes 196612
  258.1 54.0 %copy-start.3 = (f32[2,10,128,128]{2,3,0,1:T(8,128)}, f32[2,10,128,128]{2,3,0,1:T(8,128)S(1)}, u32[]{:S(2)}) copy-start(f32[2,10,128,128]{2,3,0,1:T(8,128)S(1)} %multiply_add_fusion.2) | copy-start | bytes 3932164
  312.0 9.3 %copy-start.5 = (f32[2,128,128]{2,1,0:T(8,128)}, f32[2,128,128]{2,1,0:T(8,128)S(1)}, u32[]{:S(2)}) copy-start(f32[2,128,128]{2,1,0:T(8,128)S(1)} %fusion.107) | copy-start | bytes 393220
  312.4 7.2 %copy-start.4 = (f32[2,10,128,128]{2,3,0,1:T(8,128)S(1)}, f32[2,10,128,128]{2,3,0,1:T(8,128)}, u32[]{:S(2)}) copy-start(f32[2,10,128,128]{2,3,0,1:T(8,128)} %copy-done.3) | copy-start | bytes 3932164
  319.3 47.9 %copy-start.8 = (f32[128,128]{1,0:T(8,128)S(1)}, f32[128,128]{1,0:T(8,128)}, u32[]{:S(2)}) copy-start(f32[128,128]{1,0:T(8,128)} %copy.121) | copy-start | bytes 196612
  417.8 53.5 %copy-start.6 = (f32[2,128,128]{2,1,0:T(8,128)S(1)}, f32[2,128,128]{2,1,0:T(8,128)}, u32[]{:S(2)}) copy-start(f32[2,128,128]{2,1,0:T(8,128)} %copy-done.5) | copy-start | bytes 393220
  471.6 6.1 %collective-permute-start = (bf16[2,500,16]{1,2,0:T(8,128)(2,1)S(1)}, bf16[2,500,16]{1,2,0:T(8,128)(2,1)S(1)}, u32[]{:S(2)}, u32[]{:S(2)}) collective-permute-start(bf16[2,500,16]{1,2,0:T(8,128)(2,1)S(1)} %pad_maximum_fusion.3), channel_id=1, source_target_pairs={{0,2},{2,4},{4,6},{6,8},{8,10},{10,12},{12,14},{14,16},{16,18},{18... | collective-permute-start | bytes 96008 | tf_op jit(solution)/shard_map/ppermute | solution.py:141
  477.7 6.1 %collective-permute-start.1 = (bf16[2,500,16]{1,2,0:T(8,128)(2,1)S(1)}, bf16[2,500,16]{1,2,0:T(8,128)(2,1)S(1)}, u32[]{:S(2)}, u32[]{:S(2)}) collective-permute-start(bf16[2,500,16]{1,2,0:T(8,128)(2,1)S(1)} %collective-permute-done), channel_id=1, source_target_pairs={{0,2},{2,4},{4,6},{6,8},{8,10},{10,12},{12,14},{14,16},{16,18},{18... | collective-permute-start | bytes 96008 | tf_op jit(solution)/shard_map/ppermute | solution.py:141
  477.7 6.1 %collective-permute-start.8 = (bf16[2,500,16]{1,2,0:T(8,128)(2,1)S(1)}, bf16[2,500,16]{1,2,0:T(8,128)(2,1)S(1)}, u32[]{:S(2)}, u32[]{:S(2)}) collective-permute-start(bf16[2,500,16]{1,2,0:T(8,128)(2,1)S(1)} %pad_maximum_fusion.3), channel_id=1, source_target_pairs={{0,30},{2,0},{4,2},{6,4},{8,6},{10,8},{12,10},{14,12},{16,14},{18,... | collective-permute-start | bytes 96008 | tf_op jit(solution)/shard_map/ppermute | solution.py:145
  483.8 6.0 %collective-permute-start.2 = (bf16[2,500,16]{1,2,0:T(8,128)(2,1)S(1)}, bf16[2,500,16]{1,2,0:T(8,128)(2,1)S(1)}, u32[]{:S(2)}, u32[]{:S(2)}) collective-permute-start(bf16[2,500,16]{1,2,0:T(8,128)(2,1)S(1)} %collective-permute-done.1), channel_id=1, source_target_pairs={{0,2},{2,4},{4,6},{6,8},{8,10},{10,12},{12,14},{14,16},{16,18},{18... | collective-permute-start | bytes 96008 | tf_op jit(solution)/shard_map/ppermute | solution.py:141
  483.8 6.0 %collective-permute-start.9 = (bf16[2,500,16]{1,2,0:T(8,128)(2,1)S(1)}, bf16[2,500,16]{1,2,0:T(8,128)(2,1)S(1)}, u32[]{:S(2)}, u32[]{:S(2)}) collective-permute-start(bf16[2,500,16]{1,2,0:T(8,128)(2,1)S(1)} %collective-permute-done.8), channel_id=1, source_target_pairs={{0,30},{2,0},{4,2},{6,4},{8,6},{10,8},{12,10},{14,12},{16,14},{18,... | collective-permute-start | bytes 96008 | tf_op jit(solution)/shard_map/ppermute | solution.py:145
  489.8 6.0 %collective-permute-start.3 = (bf16[2,500,16]{1,2,0:T(8,128)(2,1)S(1)}, bf16[2,500,16]{1,2,0:T(8,128)(2,1)S(1)}, u32[]{:S(2)}, u32[]{:S(2)}) collective-permute-start(bf16[2,500,16]{1,2,0:T(8,128)(2,1)S(1)} %collective-permute-done.2), channel_id=1, source_target_pairs={{0,2},{2,4},{4,6},{6,8},{8,10},{10,12},{12,14},{14,16},{16,18},{18... | collective-permute-start | bytes 96008 | tf_op jit(solution)/shard_map/ppermute | solution.py:141
  489.8 6.0 %collective-permute-start.10 = (bf16[2,500,16]{1,2,0:T(8,128)(2,1)S(1)}, bf16[2,500,16]{1,2,0:T(8,128)(2,1)S(1)}, u32[]{:S(2)}, u32[]{:S(2)}) collective-permute-start(bf16[2,500,16]{1,2,0:T(8,128)(2,1)S(1)} %collective-permute-done.9), channel_id=1, source_target_pairs={{0,30},{2,0},{4,2},{6,4},{8,6},{10,8},{12,10},{14,12},{16,14},{18,... | collective-permute-start | bytes 96008 | tf_op jit(solution)/shard_map/ppermute | solution.py:145
  495.9 6.0 %collective-permute-start.4 = (bf16[2,500,16]{1,2,0:T(8,128)(2,1)S(1)}, bf16[2,500,16]{1,2,0:T(8,128)(2,1)S(1)}, u32[]{:S(2)}, u32[]{:S(2)}) collective-permute-start(bf16[2,500,16]{1,2,0:T(8,128)(2,1)S(1)} %collective-permute-done.3), channel_id=1, source_target_pairs={{0,2},{2,4},{4,6},{6,8},{8,10},{10,12},{12,14},{14,16},{16,18},{18... | collective-permute-start | bytes 96008 | tf_op jit(solution)/shard_map/ppermute | solution.py:141
  495.9 6.0 %collective-permute-start.11 = (bf16[2,500,16]{1,2,0:T(8,128)(2,1)S(1)}, bf16[2,500,16]{1,2,0:T(8,128)(2,1)S(1)}, u32[]{:S(2)}, u32[]{:S(2)}) collective-permute-start(bf16[2,500,16]{1,2,0:T(8,128)(2,1)S(1)} %collective-permute-done.10), channel_id=1, source_target_pairs={{0,30},{2,0},{4,2},{6,4},{8,6},{10,8},{12,10},{14,12},{16,14},{18,... | collective-permute-start | bytes 96008 | tf_op jit(solution)/shard_map/ppermute | solution.py:145
  501.9 6.0 %collective-permute-start.5 = (bf16[2,500,16]{1,2,0:T(8,128)(2,1)S(1)}, bf16[2,500,16]{1,2,0:T(8,128)(2,1)S(1)}, u32[]{:S(2)}, u32[]{:S(2)}) collective-permute-start(bf16[2,500,16]{1,2,0:T(8,128)(2,1)S(1)} %collective-permute-done.4), channel_id=1, source_target_pairs={{0,2},{2,4},{4,6},{6,8},{8,10},{10,12},{12,14},{14,16},{16,18},{18... | collective-permute-start | bytes 96008 | tf_op jit(solution)/shard_map/ppermute | solution.py:141
  501.9 6.3 %collective-permute-start.12 = (bf16[2,500,16]{1,2,0:T(8,128)(2,1)S(1)}, bf16[2,500,16]{1,2,0:T(8,128)(2,1)S(1)}, u32[]{:S(2)}, u32[]{:S(2)}) collective-permute-start(bf16[2,500,16]{1,2,0:T(8,128)(2,1)S(1)} %collective-permute-done.11), channel_id=1, source_target_pairs={{0,30},{2,0},{4,2},{6,4},{8,6},{10,8},{12,10},{14,12},{16,14},{18,... | collective-permute-start | bytes 96008 | tf_op jit(solution)/shard_map/ppermute | solution.py:145
  507.9 6.3 %collective-permute-start.6 = (bf16[2,500,16]{1,2,0:T(8,128)(2,1)S(1)}, bf16[2,500,16]{1,2,0:T(8,128)(2,1)S(1)}, u32[]{:S(2)}, u32[]{:S(2)}) collective-permute-start(bf16[2,500,16]{1,2,0:T(8,128)(2,1)S(1)} %collective-permute-done.5), channel_id=1, source_target_pairs={{0,2},{2,4},{4,6},{6,8},{8,10},{10,12},{12,14},{14,16},{16,18},{18... | collective-permute-start | bytes 96008 | tf_op jit(solution)/shard_map/ppermute | solution.py:141
  508.2 6.1 %collective-permute-start.13 = (bf16[2,500,16]{1,2,0:T(8,128)(2,1)S(1)}, bf16[2,500,16]{1,2,0:T(8,128)(2,1)S(1)}, u32[]{:S(2)}, u32[]{:S(2)}) collective-permute-start(bf16[2,500,16]{1,2,0:T(8,128)(2,1)S(1)} %collective-permute-done.12), channel_id=1, source_target_pairs={{0,30},{2,0},{4,2},{6,4},{8,6},{10,8},{12,10},{14,12},{16,14},{18,... | collective-permute-start | bytes 96008 | tf_op jit(solution)/shard_map/ppermute | solution.py:145
  514.2 6.0 %collective-permute-start.7 = (bf16[2,500,16]{1,2,0:T(8,128)(2,1)S(1)}, bf16[2,500,16]{1,2,0:T(8,128)(2,1)S(1)}, u32[]{:S(2)}, u32[]{:S(2)}) collective-permute-start(bf16[2,500,16]{1,2,0:T(8,128)(2,1)S(1)} %collective-permute-done.6), channel_id=1, source_target_pairs={{0,2},{2,4},{4,6},{6,8},{8,10},{10,12},{12,14},{14,16},{16,18},{18... | collective-permute-start | bytes 96008 | tf_op jit(solution)/shard_map/ppermute | solution.py:141
  514.3 6.1 %collective-permute-start.14 = (bf16[2,500,16]{1,2,0:T(8,128)(2,1)S(1)}, bf16[2,500,16]{1,2,0:T(8,128)(2,1)S(1)}, u32[]{:S(2)}, u32[]{:S(2)}) collective-permute-start(bf16[2,500,16]{1,2,0:T(8,128)(2,1)S(1)} %collective-permute-done.13), channel_id=1, source_target_pairs={{0,30},{2,0},{4,2},{6,4},{8,6},{10,8},{12,10},{14,12},{16,14},{18,... | collective-permute-start | bytes 96008 | tf_op jit(solution)/shard_map/ppermute | solution.py:145
  522.5 0.9 copy-start.11
Sparse Core Ops, SparseCore 0:
  32.4 210.9 all-reduce.3
